TPU v7x, 256 devices: a whole 4x4x8 slice. The times are simulated.
256 devices in a mesh: tok: 32 (over z, x), head: 8 (over y, core).
Axes of the slice: x: 4, y: 4, z: 8, core: 2. Of those that a mesh axis runs over, the one named last changes fastest.
Arguments:
- embeddings: bfloat16 [4096, 4096], P('tok'), may hold values from -6 to 6
- norm_gain: bfloat16 [4096], replicated, may hold values from 0.099609375 to 1.8984375
- query_key_value_weight: bfloat16 [4096, 6144], P(None, 'head'), may hold values from -0.09375 to 0.09375
- embed_table: bfloat16 [65536, 4096], P('tok', 'head'), may hold values from -6 to 6
- rotated_cache_pages: bfloat16 [32, 32, 256, 2048], P('tok', None, None, 'head'), may hold values from -300 to 300
- page_owner_device: int32 [32, 32], P('tok'), may hold values from 0 to 31, each once within a row
- cached_length: int32 [32], P('tok'), may hold values from 2 to 8192, as said below
- vocab_shard: int32 [4096, 1], P('tok'), may hold values from 0 to 31; in each aligned block of 128 rows (0 to 127, 128 to 255, ...) at most 8 rows name the same one
- shard_row: int32 [4096], P('tok'), may hold values from 0 to 2047
- accept: int32 [4096], P('tok'), may hold values from 0 to 1, as said below
Outputs:
- out_first: bfloat16 [4096, 4096], P('tok', 'head')
- out_second: bfloat16 [4096, 4096], P('tok', 'head')
Inputs may be any that keep to these rules, and one draw needn't show every extreme that they name: `page_owner_device`: each row names every device of the tok axis once. `cached_length`: some request has exactly 8192 cached positions. `vocab_shard`: at most 8 of the 128 tokens of one request name the same shard, and some shard is named that often. `accept`: at most 32 accepted tokens in one request's block; some block has exactly 32.
All inputs are finite; a program needn't handle non-finite values.
Results may differ from a plain program's by a relative error of at most 0.017.
The roundings to bfloat16 on the way count: a program that leaves them out, or rounds other values in their place, can miss the bound.
Values may be sent and summed in bfloat16 or wider, within the bound.
No kernel may reach another device: no remote copies, remote signals or barrier semaphores. Data moves between devices by JAX's collectives and lax.ppermute only.
A program may use at most 128 MiB of HBM per device.

v0:
```python
import math

import jax
import jax.numpy as jnp
from jax import lax
from jax.experimental import pallas as pl
from jax.experimental.pallas import tpu as pltpu
from jax.sharding import PartitionSpec as P

QUERY_HEADS = 32
KEY_VALUE_HEADS = 8
HEAD_SIZE = 128
HEADS_PER_GROUP = QUERY_HEADS // KEY_VALUE_HEADS


THETA = 500000.0
KEY_CHUNK = 1024


def angles(positions):
    steps_half = jnp.arange(HEAD_SIZE // 2, dtype=jnp.float32)
    frequency = THETA ** (-(steps_half * 2.0) / HEAD_SIZE)
    return positions.astype(jnp.float32)[:, None] * frequency[None, :]


def rotate(vectors, turning):
    half_width = vectors.shape[-1] // 2
    former = vectors[..., :half_width]
    latter = vectors[..., half_width:]
    cosine = jnp.cos(turning)
    sine_of = jnp.sin(turning)
    return jnp.concatenate(
        [former * cosine - latter * sine_of, latter * cosine + former * sine_of], axis=-1
    )


def project(inputs, norm_gain, query_key_value_weight, positions):
    widened = inputs.astype(jnp.float32)
    inverse = lax.rsqrt(jnp.mean(widened * widened, axis=-1, keepdims=True) + 1e-05)
    normed = (widened * inverse * norm_gain.astype(jnp.float32)).astype(jnp.bfloat16)
    combined = jnp.dot(normed, query_key_value_weight, preferred_element_type=jnp.float32)
    rows = inputs.shape[0]
    combined = combined.reshape(rows, -1, HEADS_PER_GROUP + 2, HEAD_SIZE)
    turning = angles(positions)[:, None, None, :]
    query_vectors = rotate(combined[:, :, :HEADS_PER_GROUP], turning).astype(jnp.bfloat16)
    block_keys = rotate(combined[:, :, HEADS_PER_GROUP : HEADS_PER_GROUP + 1], turning)[
        :, :, 0
    ].astype(jnp.bfloat16)
    block_values = combined[:, :, HEADS_PER_GROUP + 1].astype(jnp.bfloat16)
    return (
        query_vectors.reshape(rows, -1),
        block_keys.reshape(rows, -1),
        block_values.reshape(rows, -1),
    )


def attention_kernel(q1_ref, q2_ref, kb1_ref, vb1_ref, kb2_ref, vb2_ref, pg_ref, us_ref,
                     o1_ref, o2_ref, s_ref):
    factor = 1.0 / math.sqrt(HEAD_SIZE)
    nt = (((1,), (1,)), ((), ()))
    rows = q1_ref.shape[0]
    q = jnp.concatenate([q1_ref[...], q2_ref[...]], axis=0)
    sb1 = lax.dot_general(q1_ref[...], kb1_ref[...], nt, preferred_element_type=jnp.float32) * factor
    sb2 = lax.dot_general(q2_ref[...], kb2_ref[...], nt, preferred_element_type=jnp.float32) * factor
    lanes = HEAD_SIZE
    high_part = jnp.concatenate([sb1, sb2], axis=0)
    keys_total = pg_ref.shape[0]
    chunks = keys_total // KEY_CHUNK
    for c in range(chunks):
        lo = c * KEY_CHUNK
        k = pg_ref[lo : lo + KEY_CHUNK, 0:HEAD_SIZE]
        sc = lax.dot_general(q, k, nt, preferred_element_type=jnp.float32) * factor
        sc = jnp.where(us_ref[:, lo : lo + KEY_CHUNK] > 0, sc, -1e30)
        s_ref[:, lo : lo + KEY_CHUNK] = sc
        for j in range(KEY_CHUNK // lanes):
            high_part = jnp.maximum(high_part, sc[:, j * lanes : (j + 1) * lanes])
    high = jnp.max(high_part, axis=1, keepdims=True)
    h1 = high[:rows]
    h2 = high[rows:]
    eb1 = jnp.exp(sb1 - h1)
    eb2 = jnp.exp(sb2 - h2)
    tot_part = jnp.concatenate([eb1, eb2], axis=0)
    acc = jnp.concatenate(
        [
            jnp.dot(eb1.astype(jnp.bfloat16), vb1_ref[...], preferred_element_type=jnp.float32),
            jnp.dot(eb2.astype(jnp.bfloat16), vb2_ref[...], preferred_element_type=jnp.float32),
        ],
        axis=0,
    )
    for c in range(chunks):
        lo = c * KEY_CHUNK
        e = jnp.exp(s_ref[:, lo : lo + KEY_CHUNK] - high)
        for j in range(KEY_CHUNK // lanes):
            tot_part = tot_part + e[:, j * lanes : (j + 1) * lanes]
        v = pg_ref[lo : lo + KEY_CHUNK, HEAD_SIZE : 2 * HEAD_SIZE]
        acc = acc + jnp.dot(e.astype(jnp.bfloat16), v, preferred_element_type=jnp.float32)
    tot = jnp.sum(tot_part, axis=1, keepdims=True)
    res = (acc / tot).astype(jnp.bfloat16)
    o1_ref[...] = res[:rows]
    o2_ref[...] = res[rows:]


def attend_both(q1, kb1, vb1, q2, kb2, vb2, pages, usable):
    rows = q1.shape[0]
    keys_total = pages.shape[0]
    qspec = pl.BlockSpec((rows, HEAD_SIZE), lambda j: (0, j))
    full = pl.BlockSpec((rows, HEAD_SIZE), lambda j: (0, 0))
    return pl.pallas_call(
        attention_kernel,
        grid=(HEADS_PER_GROUP,),
        in_specs=[
            qspec,
            qspec,
            full,
            full,
            full,
            full,
            pl.BlockSpec((keys_total, 2 * HEAD_SIZE), lambda j: (0, 0)),
            pl.BlockSpec((1, keys_total), lambda j: (0, 0)),
        ],
        out_specs=[qspec, qspec],
        out_shape=[
            jax.ShapeDtypeStruct(q1.shape, jnp.bfloat16),
            jax.ShapeDtypeStruct(q1.shape, jnp.bfloat16),
        ],
        scratch_shapes=[pltpu.VMEM((2 * rows, keys_total), jnp.float32)],
        compiler_params=pltpu.CompilerParams(vmem_limit_bytes=48 * 1024 * 1024),
    )(q1, q2, kb1, vb1, kb2, vb2, pages, usable)


def body(
    embeddings,
    norm_gain,
    query_key_value_weight,
    embed_table,
    rotated_cache_pages,
    page_owner_device,
    cached_length,
    vocab_shard,
    shard_row,
    accept,
):
    members = lax.axis_size("tok")
    length = embeddings.shape[0]
    sources = jnp.arange(members, dtype=jnp.int32)
    positions = cached_length[0] + jnp.arange(length, dtype=jnp.int32)
    page_size = rotated_cache_pages.shape[2]
    page_index = jnp.sum(
        jnp.where(page_owner_device[0][:, None] == sources[None, :], sources[:, None], 0), axis=0
    )
    page_spots = page_index[:, None] * page_size + jnp.arange(page_size, dtype=jnp.int32)[None, :]
    usable = (page_spots.reshape(1, -1) < cached_length[0]).astype(jnp.float32)

    query_vectors, block_keys, block_values = project(
        embeddings, norm_gain, query_key_value_weight, positions
    )
    target_shard = vocab_shard[:, 0]
    capacity = max(2, 2 * length // members)
    chosen = (target_shard[:, None] == sources[None, :]).astype(jnp.int32)
    earlier = (jnp.arange(length)[:, None] > jnp.arange(length)[None, :]).astype(jnp.int32)
    slot_rank = jnp.sum(jnp.dot(earlier, chosen) * chosen, axis=1)
    slot_of = target_shard * capacity + slot_rank
    slots = jnp.arange(members * capacity, dtype=jnp.int32)
    wanted = jnp.sum(
        jnp.where(slot_of[:, None] == slots[None, :], shard_row[:, None], 0), axis=0
    ).reshape(members, capacity)
    asked = lax.all_to_all(wanted, "tok", split_axis=0, concat_axis=0, tiled=True)
    found_rows = jnp.take(embed_table, asked, axis=0)
    returned = lax.all_to_all(found_rows, "tok", split_axis=0, concat_axis=0, tiled=True)
    taken = accept == 1
    most = members
    order = jnp.cumsum(taken.astype(jnp.int32)) - 1
    slots = jnp.arange(most, dtype=jnp.int32)
    hit = taken[:, None] & (order[:, None] == slots[None, :])
    token_of = jnp.sum(jnp.where(hit, jnp.arange(length, dtype=jnp.int32)[:, None], 0), axis=0)
    compact = returned[target_shard[token_of], slot_rank[token_of]]
    full_rows = lax.all_gather(compact, "head", axis=1, tiled=True)
    picked = jnp.take(full_rows, jnp.clip(order, 0, most - 1), axis=0)
    replaced = jnp.where(taken[:, None], picked, embeddings)
    arrived = lax.all_to_all(rotated_cache_pages, "tok", split_axis=1, concat_axis=0, tiled=True)
    page_size = arrived.shape[2]
    pages = arrived.reshape(members * page_size, -1)
    queries_two, keys_two, values_two = project(
        replaced, norm_gain, query_key_value_weight, positions
    )
    return attend_both(
        query_vectors, block_keys, block_values, queries_two, keys_two, values_two, pages, usable
    )


def solution(mesh):
    return jax.shard_map(
        body,
        mesh=mesh,
        in_specs=(
            P("tok", None),
            P(),
            P(None, "head"),
            P("tok", "head"),
            P("tok", None, None, "head"),
            P("tok", None),
            P("tok"),
            P("tok", None),
            P("tok"),
            P("tok"),
        ),
        out_specs=(P("tok", "head"), P("tok", "head")),
        check_vma=False,
    )
```

profile of v0, /device:TPU:28, one launch (start us, length us, event | category | flops | bytes accessed | tf_op | source)
XLA Modules:
  0.0 157.6 jit_solution(4868474294173442762)
XLA Ops:
  0.6 0.0 copy-start
  0.6 1.0 fusion.6
  1.6 0.7 fusion.40
  2.3 0.8 select_reduce_fusion
  3.1 0.1 all_to_all.20
  3.1 19.1 %all_to_all.29 = s32[32,1,8]{2,1,0:T(1,128)S(1)} all-to-all(s32[32,1,8]{2,1,0:T(1,128)S(1)} %bitcast.72), channel_id=1, replica_groups=mesh['tok'=32,'head'=8] {'tok'}, dimensions={0} | all-to-all | bytes 2048 | tf_op jit(solution)/shard_map/all_to_all | solution.py:167
  22.2 0.1 reshape.347
  22.3 0.0 copy-done
  22.4 1.2 gather_fusion
  23.5 0.1 bitcast_select_fusion
  23.6 15.1 %all_to_all.30 = bf16[32,8,512]{2,1,0:T(8,128)(2,1)S(1)} all-to-all(bf16[32,8,512]{2,1,0:T(8,128)(2,1)S(1)} %bitcast_select_fusion), channel_id=1, replica_groups=mesh['tok'=32,'head'=8] {'tok'}, dimensions={0} | all-to-all | bytes 524288 | tf_op jit(solution)/shard_map/all_to_all | solution.py:169
  38.7 0.0 copy-start.6
  38.7 0.0 copy-start.1
  38.7 0.0 copy-start.5
  38.7 0.0 copy-start.7
  38.7 6.8 %all-to-all-start.2 = ((bf16[1,32,256,256]{3,2,0,1:T(8,128)(2,1)}), bf16[1,32,256,256]{3,2,0,1:T(8,128)(2,1)}, u32[]{:S(2)}, u32[]{:S(2)}) async-start(bf16[1,32,256,256]{3,2,0,1:T(8,128)(2,1)} %bitcast.61), calls=%async_computation.2 | async-start | bytes 8388608 | tf_op jit(solution)/shard_map/all_to_all | solution.py:180
  45.5 0.0 copy-done.6
  45.5 0.1 copy.51
  45.6 0.2 reduce-window.4
  45.8 0.1 fusion.31
  45.9 0.1 select_reduce_fusion.2
  46.1 0.7 gather_fusion.2
  46.8 0.0 copy-done.1
  46.8 0.7 gather_fusion.1
  47.5 0.0 copy-done.5
  48.1 0.0 copy-done.7
  48.1 0.1 select_reduce_fusion.1
  48.2 0.1 convert_bitcast_fusion
  48.4 0.2 multiply_cosine_fusion.1
  48.6 0.7 gather_fusion.3
  49.4 13.0 %all_gather.3 = bf16[32,4096]{1,0:T(8,128)(2,1)S(1)} all-gather(bf16[32,512]{1,0:T(8,128)(2,1)S(1)} %gather_fusion.3), channel_id=1, replica_groups=mesh['tok'=32,'head'=8] {'head'}, dimensions={1}, use_global_device_ids=true | all-gather | bytes 294912 | tf_op jit(solution)/shard_map/all_gather | solution.py:177
  62.4 1.2 gather_fusion.4
  63.6 2.3 %fusion.3 = (f32[128]{0:T(128)S(1)}, bf16[128,4096]{1,0:T(8,128)(2,1)S(1)}, f32[128]{0:T(128)S(1)}) fusion(bf16[128,4096]{1,0:T(8,128)(2,1)} %param.10, bf16[128,4096]{1,0:T(8,128)(2,1)S(1)} %gather_fusion.4, pred[128]{0:T(512)(128)(4,1)S(1)} %compare_and_fusion.1, pred[128]{0:T(512)(128)(4,1)S(1)} %get-tuple-element.25), kind=kLoop, calls=%fused_computation.12 | loop fusion | flops 4194048 | bytes 3147008 | tf_op jit(solution)/shard_map/reduce_sum | solution.py:39
  65.9 0.0 copy-start.2
  65.9 5.5 %fusion.7 = f32[128,768]{0,1:T(8,128)S(1)} fusion(bf16[4096,768]{1,0:T(8,128)(2,1)} %param.12, bf16[128,4096]{1,0:T(8,128)(2,1)S(1)} %get-tuple-element.5, f32[128]{0:T(128)S(1)} %get-tuple-element.27, f32[4096]{0:T(1024)S(1)} %convert_element_type.75), kind=kOutput, calls=%fused_computation.17 | convolution fusion | flops 807403520 | bytes 7750144 | tf_op jit(solution)/shard_map/dot_general | solution.py:41
  71.4 0.0 copy-start.3
  71.4 0.7 copy-done.3
  72.2 0.1 copy.69
  72.3 0.1 copy.70
  72.4 0.0 copy-done.2
  72.4 5.4 %fusion.9 = f32[128,768]{0,1:T(8,128)S(1)} fusion(bf16[4096,768]{1,0:T(8,128)(2,1)} %param.12, bf16[128,4096]{1,0:T(8,128)(2,1)S(1)} %copy-done.2, f32[4096]{0:T(1024)S(1)} %convert_element_type.75, f32[128]{0:T(128)S(1)} %get-tuple-element.28), kind=kOutput, calls=%fused_computation.18 | convolution fusion | flops 807403520 | bytes 7750144 | tf_op jit(solution)/shard_map/dot_general | solution.py:41
  77.8 0.0 copy-start.4
  77.8 0.7 copy-done.4
  78.5 0.1 copy.66
  78.6 0.1 copy.67
  78.7 1.2 subtract_convert_fusion
  79.9 0.1 copy.63.q2_ref
  80.1 0.1 copy.62.q1_ref
  80.2 0.1 copy.71
  80.3 0.1 copy.68
  80.4 0.4 fusion.28
  80.8 0.1 maximum_bitcast_fusion.1.kb2_ref
  80.9 0.1 maximum_bitcast_fusion.kb1_ref
  81.0 57.6 %all-to-all-done.2 = bf16[1,32,256,256]{3,2,0,1:T(8,128)(2,1)} async-done(((bf16[1,32,256,256]{3,2,0,1:T(8,128)(2,1)}), bf16[1,32,256,256]{3,2,0,1:T(8,128)(2,1)}, u32[]{:S(2)}, u32[]{:S(2)}) %all-to-all-start.2) | async-done | bytes 4194336 | tf_op jit(solution)/shard_map/all_to_all | solution.py:180
  138.6 19.0 %shard_map.113 = (bf16[128,512]{1,0:T(8,128)(2,1)}, bf16[128,512]{1,0:T(8,128)(2,1)}) custom-call(bf16[128,512]{1,0:T(8,128)(2,1)S(1)} %copy.62.q1_ref, bf16[128,512]{1,0:T(8,128)(2,1)S(1)} %copy.63.q2_ref, bf16[128,128]{1,0:T(8,128)(2,1)S(1)} %maximum_bitcast_fusion.kb1_ref, bf16[128,128]{1,0:T(8,128)(2,1)S(1)} %bitcast.58, ...), custom_call_target="tpu_custom_call" | custom-call | tf_op jit(solution)/shard_map/pallas_call | solution.py:108
  (21 shorter events, 0.2 us)
Async XLA Ops:
  0.6 21.7 %copy-start = (bf16[2048,512]{1,0:T(8,128)(2,1)S(1)}, bf16[2048,512]{1,0:T(8,128)(2,1)}, u32[]{:S(2)}) copy-start(bf16[2048,512]{1,0:T(8,128)(2,1)} %param.13) | copy-start | bytes 6291460
  38.7 6.8 %copy-start.6 = (s32[128]{0:T(128)S(1)}, s32[128]{0:T(128)}, u32[]{:S(2)}) copy-start(s32[128]{0:T(128)} %param.19) | copy-start | bytes 1540
  38.7 8.0 %copy-start.1 = (s32[128,1]{0,1:T(1,128)S(1)}, s32[128,1]{0,1:T(1,128)}, u32[]{:S(2)}) copy-start(s32[128,1]{0,1:T(1,128)} %param.17) | copy-start | bytes 1540
  38.7 8.8 %copy-start.5 = (bf16[4096]{0:T(1024)(128)(2,1)S(1)}, bf16[4096]{0:T(1024)(128)(2,1)}, u32[]{:S(2)}) copy-start(bf16[4096]{0:T(1024)(128)(2,1)} %param.11) | copy-start | bytes 24580
  38.7 9.4 %copy-start.7 = (s32[1,32]{1,0:T(1,128)S(1)}, s32[1,32]{1,0:T(1,128)}, u32[]{:S(2)}) copy-start(s32[1,32]{1,0:T(1,128)} %param.15) | copy-start | bytes 388
  38.7 99.9 %all-to-all-start.2 = ((bf16[1,32,256,256]{3,2,0,1:T(8,128)(2,1)}), bf16[1,32,256,256]{3,2,0,1:T(8,128)(2,1)}, u32[]{:S(2)}, u32[]{:S(2)}) async-start(bf16[1,32,256,256]{3,2,0,1:T(8,128)(2,1)} %bitcast.61), calls=%async_computation.2 | async-start | bytes 8388608 | tf_op jit(solution)/shard_map/all_to_all | solution.py:180
  65.9 6.5 %copy-start.2 = (bf16[128,4096]{1,0:T(8,128)(2,1)S(1)}, bf16[128,4096]{1,0:T(8,128)(2,1)}, u32[]{:S(2)}) copy-start(bf16[128,4096]{1,0:T(8,128)(2,1)} %param.10) | copy-start | bytes 3145732
  71.4 0.8 copy-start.3
  77.8 0.8 copy-start.4
where the time goes:
time: 158 us
  waiting for transfers between devices  57.6 us (36%)
  blocking collectives  47.2 us (30%)
  Pallas kernels  19 us (12%)
  matrix products  11.8 us (7%)
  local copies, waits for them, and re-layouts  7.14 us (5%)
  starting transfers between devices  6.76 us (4%)
  other arithmetic  6.42 us (4%)
  between operations  1.6 us (1%)
    all_to_all x1, waiting for transfers between devices, body(): lax.all_to_all(rotated_cache_pages, 'tok', split_axis=1, concat_axis=0, t...  57.6 us
    all_to_all x1, blocking collectives, body(): lax.all_to_all(wanted, 'tok', split_axis=0, concat_axis=0, tiled=True)  19.1 us
    pallas_call x1, Pallas kernels, attend_both(): pl.pallas_call(attention_kernel, grid=(HEADS_PER_GROUP,), in_specs=[qspec...  19 us
    all_to_all x1, blocking collectives, body(): lax.all_to_all(found_rows, 'tok', split_axis=0, concat_axis=0, tiled=True)  15.1 us
    all_gather x1, blocking collectives, body(): full_rows = lax.all_gather(compact, 'head', axis=1, tiled=True)  13 us
    dot_general x2, matrix products, project(): jnp.dot(normed, query_key_value_weight, preferred_element_type=jnp.float32)  10.9 us
    all_to_all x1, starting transfers between devices, body(): lax.all_to_all(rotated_cache_pages, 'tok', split_axis=1, concat_axis=0, t...  6.76 us
  transfers between devices with their start and end apart: 1, of which 1 were waited for; matrix products, arithmetic and copies ran while one was open for 13% of the time, Pallas kernels for 0%

commit v1 on v0

--- a/solution.py
+++ b/solution.py
@@ -54,7 +54,7 @@
     )
 
 
-def attention_kernel(q1_ref, q2_ref, kb1_ref, vb1_ref, kb2_ref, vb2_ref, pg_ref, us_ref,
+def attention_kernel(full_ref, q1_ref, q2_ref, kb1_ref, vb1_ref, kb2_ref, vb2_ref, pg_ref, us_ref,
                      o1_ref, o2_ref, s_ref):
     factor = 1.0 / math.sqrt(HEAD_SIZE)
     nt = (((1,), (1,)), ((), ()))
@@ -62,24 +62,31 @@
     q = jnp.concatenate([q1_ref[...], q2_ref[...]], axis=0)
     sb1 = lax.dot_general(q1_ref[...], kb1_ref[...], nt, preferred_element_type=jnp.float32) * factor
     sb2 = lax.dot_general(q2_ref[...], kb2_ref[...], nt, preferred_element_type=jnp.float32) * factor
-    lanes = HEAD_SIZE
-    high_part = jnp.concatenate([sb1, sb2], axis=0)
+    high = jnp.concatenate(
+        [jnp.max(sb1, axis=1, keepdims=True), jnp.max(sb2, axis=1, keepdims=True)], axis=0
+    )
     keys_total = pg_ref.shape[0]
     chunks = keys_total // KEY_CHUNK
     for c in range(chunks):
         lo = c * KEY_CHUNK
         k = pg_ref[lo : lo + KEY_CHUNK, 0:HEAD_SIZE]
         sc = lax.dot_general(q, k, nt, preferred_element_type=jnp.float32) * factor
-        sc = jnp.where(us_ref[:, lo : lo + KEY_CHUNK] > 0, sc, -1e30)
         s_ref[:, lo : lo + KEY_CHUNK] = sc
-        for j in range(KEY_CHUNK // lanes):
-            high_part = jnp.maximum(high_part, sc[:, j * lanes : (j + 1) * lanes])
-    high = jnp.max(high_part, axis=1, keepdims=True)
+
+        @pl.when(full_ref[c] == 0)
+        def _():
+            s_ref[:, lo : lo + KEY_CHUNK] = jnp.where(
+                us_ref[:, lo : lo + KEY_CHUNK] > 0, s_ref[:, lo : lo + KEY_CHUNK], -1e30
+            )
+
+        high = jnp.maximum(high, jnp.max(s_ref[:, lo : lo + KEY_CHUNK], axis=1, keepdims=True))
     h1 = high[:rows]
     h2 = high[rows:]
     eb1 = jnp.exp(sb1 - h1)
     eb2 = jnp.exp(sb2 - h2)
-    tot_part = jnp.concatenate([eb1, eb2], axis=0)
+    tot = jnp.concatenate(
+        [jnp.sum(eb1, axis=1, keepdims=True), jnp.sum(eb2, axis=1, keepdims=True)], axis=0
+    )
     acc = jnp.concatenate(
         [
             jnp.dot(eb1.astype(jnp.bfloat16), vb1_ref[...], preferred_element_type=jnp.float32),
@@ -90,11 +97,9 @@
     for c in range(chunks):
         lo = c * KEY_CHUNK
         e = jnp.exp(s_ref[:, lo : lo + KEY_CHUNK] - high)
-        for j in range(KEY_CHUNK // lanes):
-            tot_part = tot_part + e[:, j * lanes : (j + 1) * lanes]
+        tot = tot + jnp.sum(e, axis=1, keepdims=True)
         v = pg_ref[lo : lo + KEY_CHUNK, HEAD_SIZE : 2 * HEAD_SIZE]
         acc = acc + jnp.dot(e.astype(jnp.bfloat16), v, preferred_element_type=jnp.float32)
-    tot = jnp.sum(tot_part, axis=1, keepdims=True)
     res = (acc / tot).astype(jnp.bfloat16)
     o1_ref[...] = res[:rows]
     o2_ref[...] = res[rows:]
@@ -103,10 +108,11 @@
 def attend_both(q1, kb1, vb1, q2, kb2, vb2, pages, usable):
     rows = q1.shape[0]
     keys_total = pages.shape[0]
-    qspec = pl.BlockSpec((rows, HEAD_SIZE), lambda j: (0, j))
-    full = pl.BlockSpec((rows, HEAD_SIZE), lambda j: (0, 0))
-    return pl.pallas_call(
-        attention_kernel,
+    qspec = pl.BlockSpec((rows, HEAD_SIZE), lambda j, f: (0, j))
+    full = pl.BlockSpec((rows, HEAD_SIZE), lambda j, f: (0, 0))
+    chunk_full = jnp.min(usable.reshape(-1, KEY_CHUNK), axis=1).astype(jnp.int32)
+    grid_spec = pltpu.PrefetchScalarGridSpec(
+        num_scalar_prefetch=1,
         grid=(HEADS_PER_GROUP,),
         in_specs=[
             qspec,
@@ -115,17 +121,21 @@
             full,
             full,
             full,
-            pl.BlockSpec((keys_total, 2 * HEAD_SIZE), lambda j: (0, 0)),
-            pl.BlockSpec((1, keys_total), lambda j: (0, 0)),
+            pl.BlockSpec((keys_total, 2 * HEAD_SIZE), lambda j, f: (0, 0)),
+            pl.BlockSpec((1, keys_total), lambda j, f: (0, 0)),
         ],
         out_specs=[qspec, qspec],
+        scratch_shapes=[pltpu.VMEM((2 * rows, keys_total), jnp.float32)],
+    )
+    return pl.pallas_call(
+        attention_kernel,
+        grid_spec=grid_spec,
         out_shape=[
             jax.ShapeDtypeStruct(q1.shape, jnp.bfloat16),
             jax.ShapeDtypeStruct(q1.shape, jnp.bfloat16),
         ],
-        scratch_shapes=[pltpu.VMEM((2 * rows, keys_total), jnp.float32)],
         compiler_params=pltpu.CompilerParams(vmem_limit_bytes=48 * 1024 * 1024),
-    )(q1, q2, kb1, vb1, kb2, vb2, pages, usable)
+    )(chunk_full, q1, q2, kb1, vb1, kb2, vb2, pages, usable)
 
 
 def body(

time: 158 us -> 165 us (1.044)
  Pallas kernels: 19 us -> 26.1 us
    pallas_call x1, Pallas kernels: 19 us -> 26.1 us  [attend_both(): pl.pallas_call(attention_kernel, grid_spec=grid_spec, out_shape=[jax.Shap...]
  transfers between devices with their start and end apart: 1 -> 1, of which waited for: 1 -> 1; matrix products, arithmetic and copies ran while one was open for 13% -> 12% of each run, Pallas kernels for 0% -> 0%
where the time goes in v1:
time: 165 us
  waiting for transfers between devices  57.4 us (35%)
  blocking collectives  47 us (28%)
  Pallas kernels  26.1 us (16%)
  matrix products  11.9 us (7%)
  local copies, waits for them, and re-layouts  7.22 us (4%)
  starting transfers between devices  6.76 us (4%)
  other arithmetic  6.74 us (4%)
    all_to_all x1, waiting for transfers between devices, body(): lax.all_to_all(rotated_cache_pages, 'tok', split_axis=1, concat_axis=0, t...  57.4 us
    pallas_call x1, Pallas kernels, attend_both(): pl.pallas_call(attention_kernel, grid_spec=grid_spec, out_shape=[jax.Shap...  26.1 us
    all_to_all x1, blocking collectives, body(): lax.all_to_all(wanted, 'tok', split_axis=0, concat_axis=0, tiled=True)  19.1 us
    all_to_all x1, blocking collectives, body(): lax.all_to_all(found_rows, 'tok', split_axis=0, concat_axis=0, tiled=True)  15.1 us
    all_gather x1, blocking collectives, body(): full_rows = lax.all_gather(compact, 'head', axis=1, tiled=True)  12.8 us
    dot_general x2, matrix products, project(): jnp.dot(normed, query_key_value_weight, preferred_element_type=jnp.float32)  10.9 us
    all_to_all x1, starting transfers between devices, body(): lax.all_to_all(rotated_cache_pages, 'tok', split_axis=1, concat_axis=0, t...  6.76 us
  transfers between devices with their start and end apart: 1, of which 1 were waited for; matrix products, arithmetic and copies ran while one was open for 12% of the time, Pallas kernels for 0%

profile of v1, /device:TPU:28, one launch (start us, length us, event | category | flops | bytes accessed | tf_op | source)
XLA Modules:
  0.0 164.7 jit_solution(12592223470052947076)
XLA Ops:
  0.6 0.0 copy-start
  0.6 1.0 fusion.6
  1.6 0.7 fusion.40
  2.3 0.8 select_reduce_fusion
  3.1 0.1 all_to_all.20
  3.1 19.1 %all_to_all.29 = s32[32,1,8]{2,1,0:T(1,128)S(1)} all-to-all(s32[32,1,8]{2,1,0:T(1,128)S(1)} %bitcast.73), channel_id=1, replica_groups=mesh['tok'=32,'head'=8] {'tok'}, dimensions={0} | all-to-all | bytes 2048 | tf_op jit(solution)/shard_map/all_to_all | solution.py:177
  22.2 0.1 reshape.351
  22.3 0.0 copy-done
  22.4 1.2 gather_fusion
  23.5 0.1 bitcast_select_fusion
  23.6 15.1 %all_to_all.30 = bf16[32,8,512]{2,1,0:T(8,128)(2,1)S(1)} all-to-all(bf16[32,8,512]{2,1,0:T(8,128)(2,1)S(1)} %bitcast_select_fusion), channel_id=1, replica_groups=mesh['tok'=32,'head'=8] {'tok'}, dimensions={0} | all-to-all | bytes 524288 | tf_op jit(solution)/shard_map/all_to_all | solution.py:179
  38.7 0.0 copy-start.6
  38.7 0.0 copy-start.1
  38.7 0.0 copy-start.5
  38.7 0.0 copy-start.7
  38.7 6.8 %all-to-all-start.2 = ((bf16[1,32,256,256]{3,2,0,1:T(8,128)(2,1)}), bf16[1,32,256,256]{3,2,0,1:T(8,128)(2,1)}, u32[]{:S(2)}, u32[]{:S(2)}) async-start(bf16[1,32,256,256]{3,2,0,1:T(8,128)(2,1)} %bitcast.62), calls=%async_computation.2 | async-start | bytes 8388608 | tf_op jit(solution)/shard_map/all_to_all | solution.py:190
  45.5 0.0 copy-done.6
  45.5 0.1 copy.51
  45.6 0.2 reduce-window.4
  45.8 0.1 fusion.31
  45.9 0.1 select_reduce_fusion.1
  46.1 0.7 gather_fusion.2
  46.8 0.0 copy-done.1
  46.8 0.7 gather_fusion.1
  47.5 0.0 copy-done.5
  48.1 0.0 copy-done.7
  48.1 0.1 select_reduce_fusion.2
  48.2 0.1 convert_bitcast_fusion
  48.4 0.2 convert_reduce_fusion
  48.5 0.1 reduce_min.14
  48.6 0.1 reduce_min.18
  48.8 0.2 multiply_cosine_fusion.1
  49.0 0.7 gather_fusion.3
  49.8 12.8 %all_gather.3 = bf16[32,4096]{1,0:T(8,128)(2,1)S(1)} all-gather(bf16[32,512]{1,0:T(8,128)(2,1)S(1)} %gather_fusion.3), channel_id=1, replica_groups=mesh['tok'=32,'head'=8] {'head'}, dimensions={1}, use_global_device_ids=true | all-gather | bytes 294912 | tf_op jit(solution)/shard_map/all_gather | solution.py:187
  62.6 1.2 gather_fusion.4
  63.8 2.3 %fusion.3 = (f32[128]{0:T(128)S(1)}, bf16[128,4096]{1,0:T(8,128)(2,1)S(1)}, f32[128]{0:T(128)S(1)}) fusion(bf16[128,4096]{1,0:T(8,128)(2,1)} %param.10, bf16[128,4096]{1,0:T(8,128)(2,1)S(1)} %gather_fusion.4, pred[128]{0:T(512)(128)(4,1)S(1)} %compare_and_fusion.1, pred[128]{0:T(512)(128)(4,1)S(1)} %get-tuple-element.25), kind=kLoop, calls=%fused_computation.12 | loop fusion | flops 4194048 | bytes 3147008 | tf_op jit(solution)/shard_map/reduce_sum | solution.py:39
  66.1 0.0 copy-start.2
  66.1 5.5 %fusion.7 = f32[128,768]{0,1:T(8,128)S(1)} fusion(bf16[4096,768]{1,0:T(8,128)(2,1)} %param.12, bf16[128,4096]{1,0:T(8,128)(2,1)S(1)} %get-tuple-element.5, f32[128]{0:T(128)S(1)} %get-tuple-element.27, f32[4096]{0:T(1024)S(1)} %convert_element_type.82), kind=kOutput, calls=%fused_computation.17 | convolution fusion | flops 807403520 | bytes 7750144 | tf_op jit(solution)/shard_map/dot_general | solution.py:41
  71.6 0.0 copy-start.3
  71.7 0.7 copy-done.3
  72.4 0.1 copy.69
  72.5 0.1 copy.70
  72.6 0.0 copy-done.2
  72.6 5.4 %fusion.9 = f32[128,768]{0,1:T(8,128)S(1)} fusion(bf16[4096,768]{1,0:T(8,128)(2,1)} %param.12, bf16[128,4096]{1,0:T(8,128)(2,1)S(1)} %copy-done.2, f32[4096]{0:T(1024)S(1)} %convert_element_type.82, f32[128]{0:T(128)S(1)} %get-tuple-element.28), kind=kOutput, calls=%fused_computation.18 | convolution fusion | flops 807403520 | bytes 7750144 | tf_op jit(solution)/shard_map/dot_general | solution.py:41
  78.0 0.0 copy-start.4
  78.0 0.7 copy-done.4
  78.8 0.1 copy.66
  78.9 0.1 copy.67
  79.0 1.2 subtract_convert_fusion
  80.2 0.1 copy.63.q2_ref
  80.3 0.1 copy.62.q1_ref
  80.4 0.1 copy.71
  80.6 0.1 copy.68
  80.7 0.4 fusion.28
  81.0 0.1 maximum_bitcast_fusion.1.kb2_ref
  81.1 0.1 maximum_bitcast_fusion.kb1_ref
  81.2 57.4 %all-to-all-done.2 = bf16[1,32,256,256]{3,2,0,1:T(8,128)(2,1)} async-done(((bf16[1,32,256,256]{3,2,0,1:T(8,128)(2,1)}), bf16[1,32,256,256]{3,2,0,1:T(8,128)(2,1)}, u32[]{:S(2)}, u32[]{:S(2)}) %all-to-all-start.2) | async-done | bytes 4194336 | tf_op jit(solution)/shard_map/all_to_all | solution.py:190
  138.6 26.1 %shard_map.113 = (bf16[128,512]{1,0:T(8,128)(2,1)}, bf16[128,512]{1,0:T(8,128)(2,1)}) custom-call(s32[8]{0:T(128)S(1)} %convert_element_type.80.full_ref, bf16[128,512]{1,0:T(8,128)(2,1)S(1)} %copy.62.q1_ref, bf16[128,512]{1,0:T(8,128)(2,1)S(1)} %copy.63.q2_ref, bf16[128,128]{1,0:T(8,128)(2,1)S(1)} %maximum_bitcast_fusion.kb1_ref, ...), custom_call_target="tpu_custom_call" | custom-call | tf_op jit(solution)/shard_map/pallas_call | solution.py:130
  (22 shorter events, 0.2 us)
Async XLA Ops:
  0.6 21.7 %copy-start = (bf16[2048,512]{1,0:T(8,128)(2,1)S(1)}, bf16[2048,512]{1,0:T(8,128)(2,1)}, u32[]{:S(2)}) copy-start(bf16[2048,512]{1,0:T(8,128)(2,1)} %param.13) | copy-start | bytes 6291460
  38.7 6.8 %copy-start.6 = (s32[128]{0:T(128)S(1)}, s32[128]{0:T(128)}, u32[]{:S(2)}) copy-start(s32[128]{0:T(128)} %param.19) | copy-start | bytes 1540
  38.7 8.0 %copy-start.1 = (s32[128,1]{0,1:T(1,128)S(1)}, s32[128,1]{0,1:T(1,128)}, u32[]{:S(2)}) copy-start(s32[128,1]{0,1:T(1,128)} %param.17) | copy-start | bytes 1540
  38.7 8.8 %copy-start.5 = (bf16[4096]{0:T(1024)(128)(2,1)S(1)}, bf16[4096]{0:T(1024)(128)(2,1)}, u32[]{:S(2)}) copy-start(bf16[4096]{0:T(1024)(128)(2,1)} %param.11) | copy-start | bytes 24580
  38.7 9.4 %copy-start.7 = (s32[1,32]{1,0:T(1,128)S(1)}, s32[1,32]{1,0:T(1,128)}, u32[]{:S(2)}) copy-start(s32[1,32]{1,0:T(1,128)} %param.15) | copy-start | bytes 388
  38.7 99.9 %all-to-all-start.2 = ((bf16[1,32,256,256]{3,2,0,1:T(8,128)(2,1)}), bf16[1,32,256,256]{3,2,0,1:T(8,128)(2,1)}, u32[]{:S(2)}, u32[]{:S(2)}) async-start(bf16[1,32,256,256]{3,2,0,1:T(8,128)(2,1)} %bitcast.62), calls=%async_computation.2 | async-start | bytes 8388608 | tf_op jit(solution)/shard_map/all_to_all | solution.py:190
  66.1 6.5 %copy-start.2 = (bf16[128,4096]{1,0:T(8,128)(2,1)S(1)}, bf16[128,4096]{1,0:T(8,128)(2,1)}, u32[]{:S(2)}) copy-start(bf16[128,4096]{1,0:T(8,128)(2,1)} %param.10) | copy-start | bytes 3145732
  71.6 0.8 copy-start.3
  78.0 0.8 copy-start.4
